TPU v7x, 128 devices: a whole 4x4x4 slice. The times are simulated.
128 devices in a mesh: dp: 32 (over y, x, core), blk: 4 (over z).
Axes of the slice: x: 4, y: 4, z: 4, core: 2. Of those that a mesh axis runs over, the one named last changes fastest.
Arguments:
- prod_feat: bfloat16 [32, 3072, 768], P('dp', 'blk'), may hold values from -23 to 23
- prec_feat: bfloat16 [32, 3072, 768], P('dp', 'blk'), may hold values from -23 to 23
- matched: int32 [32, 3072], P('dp', 'blk'), may hold values from 0 to 3071, each once within a row
- row_weight: float32 [32, 3072], P('dp', 'blk'), may hold values from 0.2 to 28, as said below
- proj_prod: bfloat16 [768, 1024], replicated, may hold values from -0.21875 to 0.21875
- proj_prec: bfloat16 [768, 1024], replicated, may hold values from -0.21875 to 0.21875
Outputs:
- loss_value: float32 [], replicated
- grad_prod: float32 [768, 1024], P('dp', 'blk')
- grad_prec: float32 [768, 1024], P('dp', 'blk')
Inputs may be any that keep to these rules, and one draw needn't show every extreme that they name: `matched`: in each of the 32 groups the 3072 values are a permutation of 0 to 3071. `row_weight`: positive.
All inputs are finite; a program needn't handle non-finite values.
Results may differ from a plain program's by a relative error of at most 0.0027.
Values may be sent and summed in bfloat16 or wider, within the bound.
No kernel may reach another device: no remote copies, remote signals or barrier semaphores. Data moves between devices by JAX's collectives and lax.ppermute only.
A program may use at most 128 MiB of HBM per device.

v0:
```python
import jax
import jax.numpy as jnp
from jax import lax
from jax.sharding import PartitionSpec as P

EPS = 1e-06
LOGIT_SCALE = 50.0


def passed_along(block, axis, distance):
    devices = range(lax.axis_size(axis))
    route = [((i - distance) % len(devices), i) for i in devices]
    return lax.ppermute(block, axis, route)


def embed_rows(features, weight):
    projected_raw = jnp.dot(features, weight, preferred_element_type=jnp.float32)
    radius = jnp.sqrt(jnp.sum(projected_raw * projected_raw, axis=1, keepdims=True) + EPS)
    unit_vec = projected_raw / radius
    return (unit_vec, unit_vec.astype(jnp.bfloat16), radius)


def similarity(queries, key_rows):
    return LOGIT_SCALE * lax.dot_general(
        queries, key_rows, (((1,), (1,)), ((), ())), preferred_element_type=jnp.float32
    )


def coefficient(scores, matches, weights, totals):
    probability = jnp.exp(scores - LOGIT_SCALE) / totals[:, None]
    return (weights[:, None] * (probability - matches.astype(jnp.float32))).astype(jnp.bfloat16)


def back_norm(unit_vec, radius, gradient):
    projected = jnp.sum(unit_vec * gradient, axis=1, keepdims=True)
    return ((gradient - unit_vec * projected) / radius).astype(jnp.bfloat16)


def per_device(prod_feat, prec_feat, matched, row_weight, proj_prod, proj_prec):
    feat_prod = prod_feat[0]
    feat_prec = prec_feat[0]
    targets = matched[0]
    weights = row_weight[0]
    row_count = feat_prod.shape[0]
    cycle_size = lax.axis_size("blk")
    cycle_pos = lax.axis_index("blk")
    unit_prod, unit16_prod, radius_prod = embed_rows(feat_prod, proj_prod)
    unit_prec, unit16_prec, radius_prec = embed_rows(feat_prec, proj_prec)
    shard_rows = lax.all_gather(unit16_prec, "blk", axis=0, tiled=True)
    scores = similarity(unit16_prod, shard_rows)
    columns = lax.iota(jnp.int32, shard_rows.shape[0])
    matches = targets[:, None] == columns[None, :]
    total_now = jnp.sum(jnp.exp(scores - LOGIT_SCALE), axis=1)
    positive_now = jnp.sum(jnp.where(matches, scores, 0.0), axis=1)
    losses = LOGIT_SCALE + jnp.log(total_now) - positive_now
    loss_local = jnp.sum(weights * losses)
    weight_local = jnp.sum(weights)
    loss_sum, weight_total = lax.psum((loss_local, weight_local), ("dp", "blk"))

    def cycle_turn(turn_index, cycle_state):
        tile_now, carried, prod_acc = cycle_state
        source = jnp.remainder(cycle_pos - turn_index, cycle_size)
        columns = source * row_count + lax.iota(jnp.int32, row_count)
        scores = similarity(unit16_prod, tile_now)
        matches = targets[:, None] == columns[None, :]
        coeffs = coefficient(scores, matches, weights, total_now)
        prod_acc = prod_acc + jnp.dot(coeffs, tile_now, preferred_element_type=jnp.float32)
        carried = carried + lax.dot_general(
            coeffs, unit16_prod, (((0,), (0,)), ((), ())), preferred_element_type=jnp.float32
        )
        tile_now = passed_along(tile_now, "blk", 1)
        carried = passed_along(carried, "blk", 1)
        return (tile_now, carried, prod_acc)

    zero_embed = jnp.zeros(unit_prec.shape, jnp.float32)
    final_state = lax.fori_loop(0, cycle_size, cycle_turn, (unit16_prec, zero_embed, zero_embed))
    prec_sum = final_state[1]
    prod_sum = final_state[2]
    dir_prod = back_norm(unit_prod, radius_prod, LOGIT_SCALE * prod_sum)
    dir_prec = back_norm(unit_prec, radius_prec, LOGIT_SCALE * prec_sum)
    head_prod = lax.dot_general(
        feat_prod, dir_prod, (((0,), (0,)), ((), ())), preferred_element_type=jnp.float32
    )
    head_prec = lax.dot_general(
        feat_prec, dir_prec, (((0,), (0,)), ((), ())), preferred_element_type=jnp.float32
    )
    head_prod = head_prod / weight_total
    head_prec = head_prec / weight_total
    partial_blk = (
        lax.psum_scatter(head_prod, "blk", scatter_dimension=1, tiled=True),
        lax.psum_scatter(head_prec, "blk", scatter_dimension=1, tiled=True),
    )
    summed_prod, summed_prec = (
        lax.psum_scatter(partial_blk[0], "dp", scatter_dimension=0, tiled=True),
        lax.psum_scatter(partial_blk[1], "dp", scatter_dimension=0, tiled=True),
    )
    return (loss_sum / weight_total, summed_prod, summed_prec)


def solution(mesh):
    placed = (P("dp", "blk", None), P("dp", "blk", None), P("dp", "blk"), P("dp", "blk"), P(), P())
    return jax.shard_map(
        per_device,
        mesh=mesh,
        in_specs=placed,
        out_specs=(P(), P("dp", "blk"), P("dp", "blk")),
        check_vma=False,
    )
```

profile of v0, /device:TPU:0, one launch (start us, length us, event | category | flops | bytes accessed | tf_op | source)
XLA Modules:
  0.0 872.1 jit_solution(11993308056530438230)
XLA Ops:
  20.2 63.0 %all-gather.2.cloned.1.call-done = bf16[3072,1024]{1,0:T(8,128)(2,1)} async-done(((bf16[768,1024]{1,0:T(8,128)(2,1)}), bf16[3072,1024]{1,0:T(8,128)(2,1)}) %all-gather.2.cloned.1.call-update) | async-done | bytes 6291472 | tf_op jit(solution)/shard_map/all_gather | solution.py:49
  83.2 9.9 %exponential_reduce_fusion = (f32[768]{0:T(1024)S(1)}, f32[768]{0:T(1024)S(1)}) fusion(s32[768]{0:T(1024)S(1)} %reduce.4, bf16[768,1024]{1,0:T(8,128)(2,1)S(1)} %fusion.14, bf16[3072,1024]{1,0:T(8,128)(2,1)} %all-gather.2.cloned.1.call-done), kind=kOutput, calls=%fused_computation.6 | convolution fusion | flops 4845991936 | bytes 7873536 | tf_op jit(solution)/shard_map/dot_general | solution.py:24
  95.2 456.2 %while.20 = (s32[]{:T(128)}, bf16[768,1024]{1,0:T(8,128)(2,1)S(1)}, f32[768,1024]{1,0:T(8,128)}, f32[768,1024]{1,0:T(8,128)}, f32[1,768]{1,0:T(1,128)S(1)}, /*in...) while((s32[]{:T(128)}, bf16[768,1024]{1,0:T(8,128)(2,1)S(1)}, ...), condition=%wide.region_9.10_spmd.clone, body=%wide.region_8.9_spmd.clone.sunk | while | flops 3630957312 | bytes 55471532 | solution.py:76
  100.2 5.4 convolution_add_fusion.2
  108.0 4.8 select_add_fusion.2
  112.8 97.8 %collective-permute-done = bf16[768,1024]{1,0:T(8,128)(2,1)S(1)} collective-permute-done((bf16[768,1024]{1,0:T(8,128)(2,1)}, bf16[768,1024]{1,0:T(8,128)(2,1)S(1)}, u32[]{:S(2)}, u32[]{:S(2)}) %collective-permute-start) | collective-permute-done | bytes 1572896 | tf_op jit(solution)/shard_map/while/body/eval_jaxpr/ppermute | solution.py:13
  211.8 3.8 multiply_convert_fusion.2
  215.6 5.4 convolution_add_fusion.2
  222.2 5.8 select_add_fusion.2
  228.0 97.1 %collective-permute-done = bf16[768,1024]{1,0:T(8,128)(2,1)S(1)} collective-permute-done((bf16[768,1024]{1,0:T(8,128)(2,1)}, bf16[768,1024]{1,0:T(8,128)(2,1)S(1)}, u32[]{:S(2)}, u32[]{:S(2)}) %collective-permute-start) | collective-permute-done | bytes 1572896 | tf_op jit(solution)/shard_map/while/body/eval_jaxpr/ppermute | solution.py:13
  326.4 3.8 multiply_convert_fusion.2
  330.1 5.4 convolution_add_fusion.2
  335.6 5.8 select_add_fusion.2
  341.4 97.3 %collective-permute-done = bf16[768,1024]{1,0:T(8,128)(2,1)S(1)} collective-permute-done((bf16[768,1024]{1,0:T(8,128)(2,1)}, bf16[768,1024]{1,0:T(8,128)(2,1)S(1)}, u32[]{:S(2)}, u32[]{:S(2)}) %collective-permute-start) | collective-permute-done | bytes 1572896 | tf_op jit(solution)/shard_map/while/body/eval_jaxpr/ppermute | solution.py:13
  443.8 5.4 convolution_add_fusion.2
  449.2 5.8 select_add_fusion.2
  455.0 96.4 %collective-permute-done = bf16[768,1024]{1,0:T(8,128)(2,1)S(1)} collective-permute-done((bf16[768,1024]{1,0:T(8,128)(2,1)}, bf16[768,1024]{1,0:T(8,128)(2,1)S(1)}, u32[]{:S(2)}, u32[]{:S(2)}) %collective-permute-start) | collective-permute-done | bytes 1572896 | tf_op jit(solution)/shard_map/while/body/eval_jaxpr/ppermute | solution.py:13
  555.5 65.3 %all-reduce = (f32[]{:T(128)}, f32[]{:T(128)}) all-reduce(f32[]{:T(128)} %multiply_reduce_fusion.4, f32[]{:T(128)} %get-tuple-element.266), channel_id=1, replica_groups=mesh['dp'=32,'blk'=4] {'dp','blk'}, use_global_device_ids=true, to_apply=%region_5.6 | all-reduce | flops 2 | bytes 16 | tf_op jit(solution)/shard_map/psum | solution.py:58
  620.9 7.0 divide_bitcast_fusion
  633.1 4.3 divide_bitcast_fusion.1
  637.4 25.1 %reduce-scatter.11.cloned.1.call-done = f32[768,256]{0,1:T(8,128)} async-done(((f32[768,1024]{0,1:T(8,128)}), f32[768,256]{0,1:T(8,128)}) %reduce-scatter.11.cloned.1.call-update) | async-done | bytes 786448 | tf_op jit(solution)/shard_map/reduce_scatter | solution.py:91
  664.9 38.1 %reduce-scatter.9.cloned.1.call-done = f32[768,256]{0,1:T(8,128)} async-done(((f32[768,1024]{0,1:T(8,128)}), f32[768,256]{0,1:T(8,128)}) %reduce-scatter.9.cloned.1.call-update) | async-done | bytes 786448 | tf_op jit(solution)/shard_map/reduce_scatter | solution.py:90
  706.7 77.1 %reduce-scatter.15.cloned.1.call-done = f32[24,256]{1,0:T(8,128)} async-done(((f32[768,256]{1,0:T(8,128)}), f32[24,256]{1,0:T(8,128)}) %reduce-scatter.15.cloned.1.call-update) | async-done | bytes 24592
  783.8 80.6 %reduce-scatter.13.cloned.1.call-done = f32[24,256]{1,0:T(8,128)} async-done(((f32[768,256]{1,0:T(8,128)}), f32[24,256]{1,0:T(8,128)}) %reduce-scatter.13.cloned.1.call-update) | async-done | bytes 24592
  (95 shorter events, 45.0 us)
Async XLA Ops:
  7.2 76.0 %all-gather.2.cloned.1.call-start = ((), (), s32[]{:S(2)}) async-start(), calls=%async_computation.4 | async-start | bytes 7864320 | tf_op jit(solution)/shard_map/all_gather | solution.py:49
  14.7 647.9 %reduce-scatter.11.cloned.1.call-start = ((), (), s32[]{:S(2)}) async-start(), calls=%async_computation.6 | async-start | bytes 3932160 | tf_op jit(solution)/shard_map/reduce_scatter | solution.py:91
  20.2 63.0 %copy-start.6 = (bf16[768,1024]{1,0:T(8,128)(2,1)}, bf16[768,1024]{1,0:T(8,128)(2,1)S(1)}, u32[]{:S(2)}) copy-start(bf16[768,1024]{1,0:T(8,128)(2,1)S(1)} %fusion.14) | copy-start | bytes 4718596
  96.4 3.8 copy-start.7
  100.2 5.5 copy-start.13
  105.6 104.9 %collective-permute-start.1 = (f32[768,1024]{1,0:T(8,128)}, f32[768,1024]{1,0:T(8,128)}, u32[]{:S(2)}, u32[]{:S(2)}) collective-permute-start(f32[768,1024]{1,0:T(8,128)} %convolution_add_fusion.2), channel_id=1, source_target_pairs={{3,0},{0,1},{1,2},{2,3},{7,4},{4,5},{5,6},{6,7},{11,8},{8,9},{9,10... | collective-permute-start | bytes 9437192 | tf_op jit(solution)/shard_map/while/body/eval_jaxpr/ppermute | solution.py:13
  106.7 103.9 %collective-permute-start = (bf16[768,1024]{1,0:T(8,128)(2,1)}, bf16[768,1024]{1,0:T(8,128)(2,1)S(1)}, u32[]{:S(2)}, u32[]{:S(2)}) collective-permute-start(bf16[768,1024]{1,0:T(8,128)(2,1)} %copy.22), channel_id=1, source_target_pairs={{3,0},{0,1},{1,2},{2,3},{7,4},{4,5},{5,6},{6,7},{11,8},{8,9},{9,10... | collective-permute-start | bytes 4718600 | tf_op jit(solution)/shard_map/while/body/eval_jaxpr/ppermute | solution.py:13
  211.8 3.8 copy-start.7
  215.6 5.5 copy-start.13
  221.1 104.1 %collective-permute-start.1 = (f32[768,1024]{1,0:T(8,128)}, f32[768,1024]{1,0:T(8,128)}, u32[]{:S(2)}, u32[]{:S(2)}) collective-permute-start(f32[768,1024]{1,0:T(8,128)} %convolution_add_fusion.2), channel_id=1, source_target_pairs={{3,0},{0,1},{1,2},{2,3},{7,4},{4,5},{5,6},{6,7},{11,8},{8,9},{9,10... | collective-permute-start | bytes 9437192 | tf_op jit(solution)/shard_map/while/body/eval_jaxpr/ppermute | solution.py:13
  221.1 104.1 %collective-permute-start = (bf16[768,1024]{1,0:T(8,128)(2,1)}, bf16[768,1024]{1,0:T(8,128)(2,1)S(1)}, u32[]{:S(2)}, u32[]{:S(2)}) collective-permute-start(bf16[768,1024]{1,0:T(8,128)(2,1)} %copy.22), channel_id=1, source_target_pairs={{3,0},{0,1},{1,2},{2,3},{7,4},{4,5},{5,6},{6,7},{11,8},{8,9},{9,10... | collective-permute-start | bytes 4718600 | tf_op jit(solution)/shard_map/while/body/eval_jaxpr/ppermute | solution.py:13
  326.4 3.8 copy-start.7
  330.1 5.5 copy-start.13
  335.6 103.1 %collective-permute-start.1 = (f32[768,1024]{1,0:T(8,128)}, f32[768,1024]{1,0:T(8,128)}, u32[]{:S(2)}, u32[]{:S(2)}) collective-permute-start(f32[768,1024]{1,0:T(8,128)} %convolution_add_fusion.2), channel_id=1, source_target_pairs={{3,0},{0,1},{1,2},{2,3},{7,4},{4,5},{5,6},{6,7},{11,8},{8,9},{9,10... | collective-permute-start | bytes 9437192 | tf_op jit(solution)/shard_map/while/body/eval_jaxpr/ppermute | solution.py:13
  335.6 103.1 %collective-permute-start = (bf16[768,1024]{1,0:T(8,128)(2,1)}, bf16[768,1024]{1,0:T(8,128)(2,1)S(1)}, u32[]{:S(2)}, u32[]{:S(2)}) collective-permute-start(bf16[768,1024]{1,0:T(8,128)(2,1)} %copy.22), channel_id=1, source_target_pairs={{3,0},{0,1},{1,2},{2,3},{7,4},{4,5},{5,6},{6,7},{11,8},{8,9},{9,10... | collective-permute-start | bytes 4718600 | tf_op jit(solution)/shard_map/while/body/eval_jaxpr/ppermute | solution.py:13
  443.7 5.5 copy-start.13
  449.2 102.2 %collective-permute-start.1 = (f32[768,1024]{1,0:T(8,128)}, f32[768,1024]{1,0:T(8,128)}, u32[]{:S(2)}, u32[]{:S(2)}) collective-permute-start(f32[768,1024]{1,0:T(8,128)} %convolution_add_fusion.2), channel_id=1, source_target_pairs={{3,0},{0,1},{1,2},{2,3},{7,4},{4,5},{5,6},{6,7},{11,8},{8,9},{9,10... | collective-permute-start | bytes 9437192 | tf_op jit(solution)/shard_map/while/body/eval_jaxpr/ppermute | solution.py:13
  449.2 102.2 %collective-permute-start = (bf16[768,1024]{1,0:T(8,128)(2,1)}, bf16[768,1024]{1,0:T(8,128)(2,1)S(1)}, u32[]{:S(2)}, u32[]{:S(2)}) collective-permute-start(bf16[768,1024]{1,0:T(8,128)(2,1)} %copy.22), channel_id=1, source_target_pairs={{3,0},{0,1},{1,2},{2,3},{7,4},{4,5},{5,6},{6,7},{11,8},{8,9},{9,10... | collective-permute-start | bytes 4718600 | tf_op jit(solution)/shard_map/while/body/eval_jaxpr/ppermute | solution.py:13
  551.4 69.4 %copy-start.11 = (bf16[1,768,768]{2,1,0:T(8,128)(2,1)S(1)}, bf16[1,768,768]{2,1,0:T(8,128)(2,1)}, u32[]{:S(2)}) copy-start(bf16[1,768,768]{2,1,0:T(8,128)(2,1)} %param.9) | copy-start | bytes 3538948
  627.9 75.1 %reduce-scatter.9.cloned.1.call-start = ((), (), s32[]{:S(2)}) async-start(), calls=%async_computation.5 | async-start | bytes 3932160 | tf_op jit(solution)/shard_map/reduce_scatter | solution.py:90
  628.0 4.0 copy-start.4
  628.0 5.1 copy-start.5
  637.4 146.4 %reduce-scatter.15.cloned.1.call-start = ((), (), s32[]{:S(2)}) async-start(), calls=%async_computation.8 | async-start | bytes 811008
  664.8 199.6 %reduce-scatter.13.cloned.1.call-start = ((), (), s32[]{:S(2)}) async-start(), calls=%async_computation.7 | async-start | bytes 811008
  (9 other events, 20.1 us)
Sparse Core Ops, SparseCore 0:
  14.8 68.3 all-gather.1
  628.1 34.4 reduce-scatter.10
  664.9 38.0 reduce-scatter.8
  706.9 76.8 reduce-scatter.14
  787.7 76.6 reduce-scatter.12
where the time goes:
time: 873 us; the launch traced here: 872 us
  waiting for transfers between devices  673 us (77%)
  matrix products  85.6 us (10%)
  blocking collectives  65.3 us (7%)
  local copies, waits for them, and re-layouts  17.7 us (2%)
  between operations  16.4 us (2%)
  other arithmetic  10.5 us (1%)
    ppermute x8, waiting for transfers between devices, passed_along(): return lax.ppermute(block, axis, route)  389 us
    unnamed x7, waiting for transfers between devices  158 us
    psum x1, blocking collectives, per_device(): loss_sum, weight_total = lax.psum((loss_local, weight_local), ('dp', 'blk'))  65.3 us
    all_gather x1, waiting for transfers between devices, per_device(): shard_rows = lax.all_gather(unit16_prec, 'blk', axis=0, tiled=True)  63 us
    reduce_scatter x1, waiting for transfers between devices, per_device(): lax.psum_scatter(head_prod, 'blk', scatter_dimension=1, tiled=True)  38.1 us
    reduce_scatter x1, waiting for transfers between devices, per_device(): lax.psum_scatter(head_prec, 'blk', scatter_dimension=1, tiled=True)  25.1 us
    dot_general x5, matrix products, similarity(): lax.dot_general(queries, key_rows, (((1,), (1,)), ((), ())), preferred_el...  24.9 us
    dot_general x4, matrix products, cycle_turn(): jnp.dot(coeffs, tile_now, preferred_element_type=jnp.float32)  22.2 us
  transfers between devices with their start and end apart: 13, of which 9 were waited for; matrix products, arithmetic and copies ran while one was open for 4% of the time, Pallas kernels for 0%

commit v1 on v0

--- a/solution.py
+++ b/solution.py
@@ -46,7 +46,12 @@
     cycle_pos = lax.axis_index("blk")
     unit_prod, unit16_prod, radius_prod = embed_rows(feat_prod, proj_prod)
     unit_prec, unit16_prec, radius_prec = embed_rows(feat_prec, proj_prec)
-    shard_rows = lax.all_gather(unit16_prec, "blk", axis=0, tiled=True)
+    ring = [unit16_prec]
+    for hop in range(3):
+        ring.append(lax.ppermute(ring[-1], "blk", [(dev, (dev + 1) % 4) for dev in range(4)]))
+    shard_rows = jnp.roll(
+        jnp.concatenate(ring[::-1], axis=0), (lax.axis_index("blk") + 1) * ring[0].shape[0], axis=0
+    )
     scores = similarity(unit16_prod, shard_rows)
     columns = lax.iota(jnp.int32, shard_rows.shape[0])
     matches = targets[:, None] == columns[None, :]

time: 873 us -> 909 us (1.041)
  waiting for transfers between devices: 673 us -> 708 us
    ppermute x0 -> x3, waiting for transfers between devices: none -> 104 us  [per_device(): lax.ppermute(ring[-1], 'blk', [(dev, (dev + 1) % 4) for dev in range(4)])]
    all_gather x1 -> x0, waiting for transfers between devices: 63 us -> none  [per_device(): shard_rows = lax.all_gather(unit16_prec, 'blk', axis=0, tiled=True)]
    unnamed x7 -> x6, waiting for transfers between devices: 158 us -> 158 us
  transfers between devices with their start and end apart: 13 -> 15, of which waited for: 9 -> 11; matrix products, arithmetic and copies ran while one was open for 4% -> 4% of each run, Pallas kernels for 0% -> 0%
where the time goes in v1:
time: 909 us; the launch traced here: 908 us
  waiting for transfers between devices  708 us (78%)
  matrix products  82.9 us (9%)
  blocking collectives  65.6 us (7%)
  local copies, waits for them, and re-layouts  22.5 us (2%)
  between operations  16.4 us (2%)
  other arithmetic  10.1 us (1%)
    ppermute x8, waiting for transfers between devices, passed_along(): return lax.ppermute(block, axis, route)  382 us
    unnamed x6, waiting for transfers between devices  158 us
    ppermute x3, waiting for transfers between devices, per_device(): lax.ppermute(ring[-1], 'blk', [(dev, (dev + 1) % 4) for dev in range(4)])  104 us
    psum x1, blocking collectives, per_device(): loss_sum, weight_total = lax.psum((loss_local, weight_local), ('dp', 'blk'))  65.6 us
    reduce_scatter x1, waiting for transfers between devices, per_device(): lax.psum_scatter(head_prod, 'blk', scatter_dimension=1, tiled=True)  38.1 us
    reduce_scatter x1, waiting for transfers between devices, per_device(): lax.psum_scatter(head_prec, 'blk', scatter_dimension=1, tiled=True)  25.2 us
    dot_general x4, matrix products, cycle_turn(): jnp.dot(coeffs, tile_now, preferred_element_type=jnp.float32)  22.3 us
    dot_general x5, matrix products, similarity(): lax.dot_general(queries, key_rows, (((1,), (1,)), ((), ())), preferred_el...  21.8 us
  transfers between devices with their start and end apart: 15, of which 11 were waited for; matrix products, arithmetic and copies ran while one was open for 4% of the time, Pallas kernels for 0%

profile of v1, /device:TPU:0, one launch (start us, length us, event | category | flops | bytes accessed | tf_op | source)
XLA Modules:
  0.0 907.8 jit_solution(8709768618779515713)
XLA Ops:
  13.9 36.5 %collective-permute-done.2 = bf16[768,1024]{1,0:T(8,128)(2,1)S(1)} collective-permute-done((bf16[768,1024]{1,0:T(8,128)(2,1)S(1)}, bf16[768,1024]{1,0:T(8,128)(2,1)S(1)}, u32[]{:S(2)}, u32[]{:S(2)}) %collective-permute-start.2) | collective-permute-done | bytes 1572896 | tf_op jit(solution)/shard_map/ppermute | solution.py:51
  51.5 35.8 %collective-permute-done.3 = bf16[768,1024]{1,0:T(8,128)(2,1)} collective-permute-done((bf16[768,1024]{1,0:T(8,128)(2,1)S(1)}, bf16[768,1024]{1,0:T(8,128)(2,1)}, u32[]{:S(2)}, u32[]{:S(2)}) %collective-permute-start.3) | collective-permute-done | bytes 1572896 | tf_op jit(solution)/shard_map/ppermute | solution.py:51
  91.6 31.8 %collective-permute-done.4 = bf16[768,1024]{1,0:T(8,128)(2,1)} collective-permute-done((bf16[768,1024]{1,0:T(8,128)(2,1)}, bf16[768,1024]{1,0:T(8,128)(2,1)}, u32[]{:S(2)}, u32[]{:S(2)}) %collective-permute-start.4) | collective-permute-done | bytes 1572896 | tf_op jit(solution)/shard_map/ppermute | solution.py:51
  131.4 6.8 exponential_reduce_fusion
  140.2 446.5 %while.20 = (s32[]{:T(128)}, bf16[768,1024]{1,0:T(8,128)(2,1)S(1)}, f32[768,1024]{1,0:T(8,128)}, f32[768,1024]{1,0:T(8,128)}, f32[1,768]{1,0:T(1,128)S(1)}, /*in...) while((s32[]{:T(128)}, bf16[768,1024]{1,0:T(8,128)(2,1)S(1)}, ...), condition=%wide.region_9.10_spmd.clone, body=%wide.region_8.9_spmd.clone.sunk | while | flops 3630957312 | bytes 55471532 | solution.py:81
  145.2 5.4 convolution_add_fusion.2
  150.6 4.9 select_add_fusion.2
  155.5 97.7 %collective-permute-done = bf16[768,1024]{1,0:T(8,128)(2,1)S(1)} collective-permute-done((bf16[768,1024]{1,0:T(8,128)(2,1)}, bf16[768,1024]{1,0:T(8,128)(2,1)S(1)}, u32[]{:S(2)}, u32[]{:S(2)}) %collective-permute-start) | collective-permute-done | bytes 1572896 | tf_op jit(solution)/shard_map/while/body/eval_jaxpr/ppermute | solution.py:13
  258.2 5.4 convolution_add_fusion.2
  263.7 5.8 select_add_fusion.2
  269.5 95.8 %collective-permute-done = bf16[768,1024]{1,0:T(8,128)(2,1)S(1)} collective-permute-done((bf16[768,1024]{1,0:T(8,128)(2,1)}, bf16[768,1024]{1,0:T(8,128)(2,1)S(1)}, u32[]{:S(2)}, u32[]{:S(2)}) %collective-permute-start) | collective-permute-done | bytes 1572896 | tf_op jit(solution)/shard_map/while/body/eval_jaxpr/ppermute | solution.py:13
  370.3 5.4 convolution_add_fusion.2
  375.7 5.8 select_add_fusion.2
  381.6 94.9 %collective-permute-done = bf16[768,1024]{1,0:T(8,128)(2,1)S(1)} collective-permute-done((bf16[768,1024]{1,0:T(8,128)(2,1)}, bf16[768,1024]{1,0:T(8,128)(2,1)S(1)}, u32[]{:S(2)}, u32[]{:S(2)}) %collective-permute-start) | collective-permute-done | bytes 1572896 | tf_op jit(solution)/shard_map/while/body/eval_jaxpr/ppermute | solution.py:13
  481.5 5.4 convolution_add_fusion.2
  486.9 5.8 select_add_fusion.2
  492.7 94.0 %collective-permute-done = bf16[768,1024]{1,0:T(8,128)(2,1)S(1)} collective-permute-done((bf16[768,1024]{1,0:T(8,128)(2,1)}, bf16[768,1024]{1,0:T(8,128)(2,1)S(1)}, u32[]{:S(2)}, u32[]{:S(2)}) %collective-permute-start) | collective-permute-done | bytes 1572896 | tf_op jit(solution)/shard_map/while/body/eval_jaxpr/ppermute | solution.py:13
  590.8 65.6 %all-reduce = (f32[]{:T(128)}, f32[]{:T(128)}) all-reduce(f32[]{:T(128)} %multiply_reduce_fusion.4, f32[]{:T(128)} %get-tuple-element.266), channel_id=1, replica_groups=mesh['dp'=32,'blk'=4] {'dp','blk'}, use_global_device_ids=true, to_apply=%region_5.6 | all-reduce | flops 2 | bytes 16 | tf_op jit(solution)/shard_map/psum | solution.py:63
  656.4 7.0 divide_bitcast_fusion
  668.6 4.2 divide_bitcast_fusion.1
  672.9 25.2 %reduce-scatter.11.cloned.1.call-done = f32[768,256]{0,1:T(8,128)} async-done(((f32[768,1024]{0,1:T(8,128)}), f32[768,256]{0,1:T(8,128)}) %reduce-scatter.11.cloned.1.call-update) | async-done | bytes 786448 | tf_op jit(solution)/shard_map/reduce_scatter | solution.py:96
  700.5 38.1 %reduce-scatter.9.cloned.1.call-done = f32[768,256]{0,1:T(8,128)} async-done(((f32[768,1024]{0,1:T(8,128)}), f32[768,256]{0,1:T(8,128)}) %reduce-scatter.9.cloned.1.call-update) | async-done | bytes 786448 | tf_op jit(solution)/shard_map/reduce_scatter | solution.py:95
  742.2 77.3 %reduce-scatter.15.cloned.1.call-done = f32[24,256]{1,0:T(8,128)} async-done(((f32[768,256]{1,0:T(8,128)}), f32[24,256]{1,0:T(8,128)}) %reduce-scatter.15.cloned.1.call-update) | async-done | bytes 24592
  819.5 80.6 %reduce-scatter.13.cloned.1.call-done = f32[24,256]{1,0:T(8,128)} async-done(((f32[768,256]{1,0:T(8,128)}), f32[24,256]{1,0:T(8,128)}) %reduce-scatter.13.cloned.1.call-update) | async-done | bytes 24592
  (108 shorter events, 55.9 us)
Async XLA Ops:
  7.2 690.9 %reduce-scatter.11.cloned.1.call-start = ((), (), s32[]{:S(2)}) async-start(), calls=%async_computation.5 | async-start | bytes 3932160 | tf_op jit(solution)/shard_map/reduce_scatter | solution.py:96
  11.3 39.1 %copy-start.1 = (f32[768,1024]{1,0:T(8,128)}, f32[768,1024]{1,0:T(8,128)S(1)}, u32[]{:S(2)}) copy-start(f32[768,1024]{1,0:T(8,128)S(1)} %get-tuple-element.291) | copy-start | bytes 9437188
  11.3 76.0 %copy-start.11 = (s32[1,768]{1,0:T(1,128)S(1)}, s32[1,768]{1,0:T(1,128)}, u32[]{:S(2)}) copy-start(s32[1,768]{1,0:T(1,128)} %param.10) | copy-start | bytes 9220
  11.3 76.0 %copy-start.10 = (f32[1,768]{1,0:T(1,128)S(1)}, f32[1,768]{1,0:T(1,128)}, u32[]{:S(2)}) copy-start(f32[1,768]{1,0:T(1,128)} %param.11) | copy-start | bytes 9220
  11.8 38.6 %collective-permute-start.2 = (bf16[768,1024]{1,0:T(8,128)(2,1)S(1)}, bf16[768,1024]{1,0:T(8,128)(2,1)S(1)}, u32[]{:S(2)}, u32[]{:S(2)}) collective-permute-start(bf16[768,1024]{1,0:T(8,128)(2,1)S(1)} %fusion.18), channel_id=1, source_target_pairs={{0,1},{1,2},{2,3},{3,0},{4,5},{5,6},{6,7},{7,4},{8,9},{9,10},{10,1... | collective-permute-start | bytes 4718600 | tf_op jit(solution)/shard_map/ppermute | solution.py:51
  50.4 36.9 %collective-permute-start.3 = (bf16[768,1024]{1,0:T(8,128)(2,1)S(1)}, bf16[768,1024]{1,0:T(8,128)(2,1)}, u32[]{:S(2)}, u32[]{:S(2)}) collective-permute-start(bf16[768,1024]{1,0:T(8,128)(2,1)S(1)} %collective-permute-done.2), channel_id=1, source_target_pairs={{0,1},{1,2},{2,3},{3,0},{4,5},{5,6},{6,7},{7,4},{8,9},{9,10},{10,1... | collective-permute-start | bytes 4718600 | tf_op jit(solution)/shard_map/ppermute | solution.py:51
  87.3 36.2 %collective-permute-start.4 = (bf16[768,1024]{1,0:T(8,128)(2,1)}, bf16[768,1024]{1,0:T(8,128)(2,1)}, u32[]{:S(2)}, u32[]{:S(2)}) collective-permute-start(bf16[768,1024]{1,0:T(8,128)(2,1)} %collective-permute-done.3), channel_id=1, source_target_pairs={{0,1},{1,2},{2,3},{3,0},{4,5},{5,6},{6,7},{7,4},{8,9},{9,10},{10,1... | collective-permute-start | bytes 4718600 | tf_op jit(solution)/shard_map/ppermute | solution.py:51
  91.2 32.3 %copy-start.3 = (f32[768,1024]{1,0:T(8,128)}, f32[768,1024]{1,0:T(8,128)S(1)}, u32[]{:S(2)}) copy-start(f32[768,1024]{1,0:T(8,128)S(1)} %get-tuple-element.289) | copy-start | bytes 9437188
  91.6 39.7 %copy-start.8 = (bf16[768,1024]{1,0:T(8,128)(2,1)}, bf16[768,1024]{1,0:T(8,128)(2,1)S(1)}, u32[]{:S(2)}) copy-start(bf16[768,1024]{1,0:T(8,128)(2,1)S(1)} %fusion.17) | copy-start | bytes 4718596
  91.6 35.1 %copy-start.6 = (bf16[768,1024]{1,0:T(8,128)(2,1)S(1)}, bf16[768,1024]{1,0:T(8,128)(2,1)}, u32[]{:S(2)}) copy-start(bf16[768,1024]{1,0:T(8,128)(2,1)} %copy-done.5) | copy-start | bytes 4718596
  150.6 102.6 %collective-permute-start.1 = (f32[768,1024]{1,0:T(8,128)}, f32[768,1024]{1,0:T(8,128)}, u32[]{:S(2)}, u32[]{:S(2)}) collective-permute-start(f32[768,1024]{1,0:T(8,128)} %convolution_add_fusion.2), channel_id=1, source_target_pairs={{3,0},{0,1},{1,2},{2,3},{7,4},{4,5},{5,6},{6,7},{11,8},{8,9},{9,10... | collective-permute-start | bytes 9437192 | tf_op jit(solution)/shard_map/while/body/eval_jaxpr/ppermute | solution.py:13
  150.6 102.6 %collective-permute-start = (bf16[768,1024]{1,0:T(8,128)(2,1)}, bf16[768,1024]{1,0:T(8,128)(2,1)S(1)}, u32[]{:S(2)}, u32[]{:S(2)}) collective-permute-start(bf16[768,1024]{1,0:T(8,128)(2,1)} %copy.29), channel_id=1, source_target_pairs={{3,0},{0,1},{1,2},{2,3},{7,4},{4,5},{5,6},{6,7},{11,8},{8,9},{9,10... | collective-permute-start | bytes 4718600 | tf_op jit(solution)/shard_map/while/body/eval_jaxpr/ppermute | solution.py:13
  263.6 101.6 %collective-permute-start.1 = (f32[768,1024]{1,0:T(8,128)}, f32[768,1024]{1,0:T(8,128)}, u32[]{:S(2)}, u32[]{:S(2)}) collective-permute-start(f32[768,1024]{1,0:T(8,128)} %convolution_add_fusion.2), channel_id=1, source_target_pairs={{3,0},{0,1},{1,2},{2,3},{7,4},{4,5},{5,6},{6,7},{11,8},{8,9},{9,10... | collective-permute-start | bytes 9437192 | tf_op jit(solution)/shard_map/while/body/eval_jaxpr/ppermute | solution.py:13
  263.6 101.6 %collective-permute-start = (bf16[768,1024]{1,0:T(8,128)(2,1)}, bf16[768,1024]{1,0:T(8,128)(2,1)S(1)}, u32[]{:S(2)}, u32[]{:S(2)}) collective-permute-start(bf16[768,1024]{1,0:T(8,128)(2,1)} %copy.29), channel_id=1, source_target_pairs={{3,0},{0,1},{1,2},{2,3},{7,4},{4,5},{5,6},{6,7},{11,8},{8,9},{9,10... | collective-permute-start | bytes 4718600 | tf_op jit(solution)/shard_map/while/body/eval_jaxpr/ppermute | solution.py:13
  370.3 5.4 copy-start.14
  375.7 100.7 %collective-permute-start.1 = (f32[768,1024]{1,0:T(8,128)}, f32[768,1024]{1,0:T(8,128)}, u32[]{:S(2)}, u32[]{:S(2)}) collective-permute-start(f32[768,1024]{1,0:T(8,128)} %convolution_add_fusion.2), channel_id=1, source_target_pairs={{3,0},{0,1},{1,2},{2,3},{7,4},{4,5},{5,6},{6,7},{11,8},{8,9},{9,10... | collective-permute-start | bytes 9437192 | tf_op jit(solution)/shard_map/while/body/eval_jaxpr/ppermute | solution.py:13
  375.7 100.7 %collective-permute-start = (bf16[768,1024]{1,0:T(8,128)(2,1)}, bf16[768,1024]{1,0:T(8,128)(2,1)S(1)}, u32[]{:S(2)}, u32[]{:S(2)}) collective-permute-start(bf16[768,1024]{1,0:T(8,128)(2,1)} %copy.29), channel_id=1, source_target_pairs={{3,0},{0,1},{1,2},{2,3},{7,4},{4,5},{5,6},{6,7},{11,8},{8,9},{9,10... | collective-permute-start | bytes 4718600 | tf_op jit(solution)/shard_map/while/body/eval_jaxpr/ppermute | solution.py:13
  481.5 5.4 copy-start.14
  486.9 99.8 %collective-permute-start.1 = (f32[768,1024]{1,0:T(8,128)}, f32[768,1024]{1,0:T(8,128)}, u32[]{:S(2)}, u32[]{:S(2)}) collective-permute-start(f32[768,1024]{1,0:T(8,128)} %convolution_add_fusion.2), channel_id=1, source_target_pairs={{3,0},{0,1},{1,2},{2,3},{7,4},{4,5},{5,6},{6,7},{11,8},{8,9},{9,10... | collective-permute-start | bytes 9437192 | tf_op jit(solution)/shard_map/while/body/eval_jaxpr/ppermute | solution.py:13
  486.9 99.8 %collective-permute-start = (bf16[768,1024]{1,0:T(8,128)(2,1)}, bf16[768,1024]{1,0:T(8,128)(2,1)S(1)}, u32[]{:S(2)}, u32[]{:S(2)}) collective-permute-start(bf16[768,1024]{1,0:T(8,128)(2,1)} %copy.29), channel_id=1, source_target_pairs={{3,0},{0,1},{1,2},{2,3},{7,4},{4,5},{5,6},{6,7},{11,8},{8,9},{9,10... | collective-permute-start | bytes 4718600 | tf_op jit(solution)/shard_map/while/body/eval_jaxpr/ppermute | solution.py:13
  586.7 69.7 %copy-start.12 = (bf16[1,768,768]{2,1,0:T(8,128)(2,1)S(1)}, bf16[1,768,768]{2,1,0:T(8,128)(2,1)}, u32[]{:S(2)}) copy-start(bf16[1,768,768]{2,1,0:T(8,128)(2,1)} %param.9) | copy-start | bytes 3538948
  663.4 75.1 %reduce-scatter.9.cloned.1.call-start = ((), (), s32[]{:S(2)}) async-start(), calls=%async_computation.4 | async-start | bytes 3932160 | tf_op jit(solution)/shard_map/reduce_scatter | solution.py:95
  672.8 146.7 %reduce-scatter.15.cloned.1.call-start = ((), (), s32[]{:S(2)}) async-start(), calls=%async_computation.7 | async-start | bytes 811008
  700.4 199.7 %reduce-scatter.13.cloned.1.call-start = ((), (), s32[]{:S(2)}) async-start(), calls=%async_computation.6 | async-start | bytes 811008
  (12 other events, 43.7 us)
Sparse Core Ops, SparseCore 0:
  663.6 34.4 reduce-scatter.10
  700.5 38.0 reduce-scatter.8
  742.6 76.8 reduce-scatter.14
  823.4 76.6 reduce-scatter.12
